TPU v7x, 32 devices: a whole 2x2x4 slice. The times are simulated.
32 devices in a mesh: swath: 2 (over y), sub: 4 (over z), beam: 2 (over x), half: 2 (over core).
Axes of the slice: x: 2, y: 2, z: 4, core: 2. Of those that a mesh axis runs over, the one named last changes fastest.
Arguments:
- images: bfloat16 [4, 2, 2048, 1024], P('sub', None, ('swath', 'half'), 'beam'), parts along dimension 2, may hold values from -6 to 6
- offsets: float32 [4], replicated, may hold values from 3840 to 4505
- owners: int32 [2, 4], replicated, may hold values from 0 to 3, each once within a row
Outputs:
- sectors: bfloat16 [8, 1, 2, 512, 2048], P(('sub', 'beam'), None, None, None, ('swath', 'half')), parts along dimension 4
There are 2 independent parts, one for each index of `swath`. A program takes and returns all parts, laid end to end along the dimension named above; an argument that names none is the same for every part. Nothing has to cross between parts.
Inputs may be any that keep to these rules, and one draw needn't show every extreme that they name: Each row of owners names every one of the 4 sectors of its beam shard exactly once.
All inputs are finite; a program needn't handle non-finite values.
Results may differ from a plain program's by a relative error of at most 0.0052.
Values may be sent and summed in bfloat16 or wider, within the bound.
No kernel may reach another device: no remote copies, remote signals or barrier semaphores. Data moves between devices by JAX's collectives and lax.ppermute only.
A program may use at most 64 MiB of HBM per device.

v0:
```python
import math
import jax
import numpy as np
import jax.numpy as jnp
from jax import lax
from jax.sharding import PartitionSpec as P

B = 1024
NR = 1024


def swapped(value, axis, distance):
    return lax.ppermute(value, axis, [(i, i ^ 1 << distance) for i in range(lax.axis_size(axis))])


def odd_kernel(beam_total, columns):
    spacing = (
        np.arange(columns, dtype=np.int64)[None, :] - np.arange(beam_total, dtype=np.int64)[:, None]
    )
    parity = np.where(spacing % 2 == 0, 1.0, -1.0).astype(np.float32)
    angles = (2.0 * spacing.astype(np.float32) + np.float32(1.0)) * np.float32(
        math.pi / (2.0 * beam_total)
    )
    values = parity * np.cos(angles) / (np.float32(beam_total) * np.sin(angles))
    return jnp.asarray(values.astype(np.float32).astype(jnp.bfloat16))


def steer_phase(upsampled, shifts, rows_at, beams_at, beams_out):
    ratios = NR / (NR + rows_at.astype(jnp.float32))
    tilts = (2.0 * beams_at.astype(jnp.float32) + 1.0) / beams_out - 1.0
    phases = ratios[:, None] * tilts[None, :] * shifts[..., None, None]
    cosine = jnp.cos(phases)
    sines = jnp.sin(phases)
    real_part = upsampled[..., 0, :, :]
    imag_part = upsampled[..., 1, :, :]
    return jnp.stack(
        [real_part * cosine - imag_part * sines, real_part * sines + imag_part * cosine], -3
    )


def rotate_sum(children, odd_beams, shifts, rows_at, beams_out):
    count = children.shape[-1]
    even_at = 2 * jnp.arange(count, dtype=jnp.int32)
    even_sum = jnp.sum(
        steer_phase(children.astype(jnp.float32), shifts, rows_at, even_at, beams_out), axis=0
    )
    odd_sum = jnp.sum(steer_phase(odd_beams, shifts, rows_at, even_at + 1, beams_out), axis=0)
    joined = jnp.stack([even_sum, odd_sum], -1)
    return joined.reshape(even_sum.shape[:-1] + (2 * count,)).astype(jnp.bfloat16)


def odd_local(children, kernel):
    product = jnp.dot(
        children.reshape(-1, children.shape[-1]), kernel, preferred_element_type=jnp.float32
    )
    return product.reshape(children.shape[:-1] + (kernel.shape[1],))


def swap_first(pieces):
    return swapped(pieces, "sub", 0)


def swap_second(pieces):
    return swapped(pieces, "sub", 1)


def keep_and_trade(field, which_bit, swapper):
    length = field.shape[2] // 2
    kept = lax.dynamic_slice_in_dim(field, which_bit * length, length, 2)
    given = lax.dynamic_slice_in_dim(field, (1 - which_bit) * length, length, 2)
    return (jnp.stack([kept, swapper(given)]), length)


def shift_block(offsets, index, per_device):
    return lax.dynamic_slice_in_dim(offsets, index * per_device, per_device, 0)


def body(images, offsets, owners):
    sub_count = lax.axis_size("sub")
    beam_count = lax.axis_size("beam")
    sub_place = lax.axis_index("sub")
    beam_lane = lax.axis_index("beam")
    half_side = lax.axis_index("half")
    low_bit = sub_place % 2
    high_bit = sub_place // 2 % 2
    per_device = images.shape[0]
    half_rows = images.shape[2]
    own_shift = shift_block(offsets, sub_place, per_device)
    mate_shift = shift_block(offsets, jnp.bitwise_xor(sub_place, 1), per_device)
    shifts_one = jnp.stack([own_shift, mate_shift])
    pair_base = sub_place - low_bit
    mate_base = jnp.bitwise_xor(sub_place, 2) - low_bit
    center_own = (
        shift_block(offsets, pair_base, per_device)
        + shift_block(offsets, pair_base + 1, per_device)
    ) * 0.5
    center_mate = (
        shift_block(offsets, mate_base, per_device)
        + shift_block(offsets, mate_base + 1, per_device)
    ) * 0.5
    shifts_two = jnp.stack([center_own, center_mate])
    all_beams = lax.all_to_all(images, "beam", split_axis=2, concat_axis=3, tiled=True)
    block_rows = all_beams.shape[2]
    start_row = half_side * half_rows + beam_lane * block_rows
    children, length = keep_and_trade(all_beams, low_bit, swap_first)
    rows_at = start_row + low_bit * length + jnp.arange(length, dtype=jnp.int32)
    odd_beams = odd_local(children, odd_kernel(B, B))
    first_merge = rotate_sum(children, odd_beams, shifts_one, rows_at, 2 * B)
    children, quarter = keep_and_trade(first_merge, high_bit, swap_second)
    rows_at = (
        start_row + low_bit * length + high_bit * quarter + jnp.arange(quarter, dtype=jnp.int32)
    )
    odd_beams = odd_local(children, odd_kernel(2 * B, 2 * B))
    merged = rotate_sum(children, odd_beams, shifts_two, rows_at, 4 * B)
    sector_tiles = merged.reshape(per_device, 2, quarter, beam_count, sub_count, -1)
    beam_ids = jnp.arange(beam_count, dtype=jnp.int32)[:, None]
    picked = sector_tiles[:, :, :, beam_ids, owners, :]
    outgoing = picked.transpose(4, 3, 0, 1, 5, 2)
    received = lax.all_to_all(
        lax.all_to_all(outgoing, "sub", split_axis=0, concat_axis=0, tiled=True),
        "beam",
        split_axis=1,
        concat_axis=1,
        tiled=True,
    )
    sector_width = received.shape[4]
    received = received.reshape(
        sub_count // 4, 2, 2, beam_count, per_device, 2, sector_width, quarter
    )
    received = received.transpose(0, 4, 5, 6, 3, 2, 1, 7)
    return received.reshape(1, sub_count // 4 * per_device, 2, sector_width, half_rows)


def solution(mesh):
    placed = (P("sub", None, ("swath", "half"), "beam"), P(), P())
    return jax.shard_map(
        body,
        mesh=mesh,
        in_specs=placed,
        out_specs=P(("sub", "beam"), None, None, None, ("swath", "half")),
        check_vma=False,
    )
```

profile of v0, /device:TPU:0, one launch (start us, length us, event | category | flops | bytes accessed | tf_op | source)
XLA Modules:
  0.0 138.8 jit_solution(17803852248841441353)
XLA Ops:
  0.0 0.0 copy-start
  0.0 3.3 %copy.34 = bf16[1,2,512,512]{3,1,0,2:T(2,128)(2,1)} copy(bf16[1,2,512,512]{3,2,1,0:T(8,128)(2,1)} %param.5) | data formatting | bytes 2097152 | tf_op args[0]
  3.3 4.2 %all-to-all-start = ((bf16[1,2,512,512]{3,1,0,2:T(2,128)(2,1)}), bf16[1,2,512,512]{3,1,0,2:T(2,128)(2,1)S(1)}, u32[]{:S(2)}, u32[]{:S(2)}) async-start(bf16[1,2,512,512]{3,1,0,2:T(2,128)(2,1)} %copy.34), calls=%async_computation | async-start | bytes 2097152 | tf_op jit(solution)/shard_map/all_to_all | solution.py:102
  7.5 0.0 copy-done
  7.5 0.7 fusion.34
  8.3 13.7 %all-to-all-done = bf16[1,2,512,512]{3,1,0,2:T(2,128)(2,1)S(1)} async-done(((bf16[1,2,512,512]{3,1,0,2:T(2,128)(2,1)}), bf16[1,2,512,512]{3,1,0,2:T(2,128)(2,1)S(1)}, u32[]{:S(2)}, u32[]{:S(2)}) %all-to-all-start) | async-done | bytes 1048608 | tf_op jit(solution)/shard_map/all_to_all | solution.py:102
  22.0 1.1 copy.52
  23.0 0.0 copy-start.1
  23.1 0.8 all_to_all.22
  23.8 0.1 dynamic-slice_bitcast_fusion
  23.9 1.9 %collective-permute-start = (bf16[1,2,128,1024]{3,2,1,0:T(8,128)(2,1)S(1)}, bf16[1,2,128,1024]{3,2,1,0:T(8,128)(2,1)S(1)}, u32[]{:S(2)}, u32[]{:S(2)}) collective-permute-start(bf16[1,2,128,1024]{3,2,1,0:T(8,128)(2,1)S(1)} %get-tuple-element.16), channel_id=1, source_target_pairs={{0,4},{4,0},{8,12},{12,8},{1,5},{5,1},{9,13},{13,9},{2,6},{6,2},{1... | collective-permute-start | bytes 1572872 | tf_op jit(solution)/shard_map/ppermute | solution.py:13
  25.8 1.4 maximum_bitcast_fusion
  29.6 0.0 copy-done.1
  29.6 0.0 copy-start.2
  29.7 0.1 broadcast_multiply_fusion.3
  29.8 7.3 %collective-permute-done = bf16[1,2,128,1024]{3,2,1,0:T(8,128)(2,1)S(1)} collective-permute-done((bf16[1,2,128,1024]{3,2,1,0:T(8,128)(2,1)S(1)}, bf16[1,2,128,1024]{3,2,1,0:T(8,128)(2,1)S(1)}, u32[]{:S(2)}, u32[]{:S(2)}) %collective-permute-start) | collective-permute-done | bytes 524320 | tf_op jit(solution)/shard_map/ppermute | solution.py:13
  37.1 0.1 fusion.27
  37.2 0.0 copy-done.2
  37.2 1.3 convolution_bitcast_fusion.1
  38.5 8.0 %fusion.22 = (f32[2,1,1,128,1024]{4,3,2,0,1:T(8,128)S(1)}, f32[2,1,1,128,1024]{4,3,2,0,1:T(8,128)S(1)}, f32[2,1,1,128,1024]{4,3,2,0,1:T(8,128)S(1)}, f32[2,1,1,128,1024]{4,3,2,0,1:T(8,128)S(1)}) fusion(f32[2,1,2,128,1024]{4,3,2,0,1:T(8,128)S(1)} %fusion.27, f32[2]{0:T(128)S(1)} %maximum_bitcast_fusion, f32[128,1024]{1,0:T(8,128)S(1)} %get-tuple-element.29, ...), kind=kLoop, calls=%fused_computation.37 | loop fusion | flops 3670016 | bytes 9437192 | tf_op jit(solution)/shard_map/sub | solution.py:37
  46.5 0.1 maximum_reduce_fusion
  46.7 0.1 maximum_reduce_fusion.1
  46.8 0.1 pad_maximum_fusion.1
  46.9 0.8 copy.36
  47.7 0.6 constant_dynamic-slice_fusion.1
  48.4 1.1 copy.48
  49.5 2.6 %collective-permute-start.1 = (bf16[1,2,64,2048]{3,2,1,0:T(8,128)(2,1)}, bf16[1,2,64,2048]{3,2,1,0:T(8,128)(2,1)S(1)}, u32[]{:S(2)}, u32[]{:S(2)}) collective-permute-start(bf16[1,2,64,2048]{3,2,1,0:T(8,128)(2,1)} %copy.48), channel_id=1, source_target_pairs={{0,8},{4,12},{8,0},{12,4},{1,9},{5,13},{9,1},{13,5},{2,10},{6,14},... | collective-permute-start | bytes 1572872 | tf_op jit(solution)/shard_map/ppermute | solution.py:13
  52.1 0.1 maximum_bitcast_fusion.1
  52.1 0.1 reshape.414
  52.2 0.2 broadcast_multiply_fusion.1
  52.4 0.3 copy.37
  52.7 21.4 %collective-permute-done.1 = bf16[1,2,64,2048]{3,2,1,0:T(8,128)(2,1)S(1)} collective-permute-done((bf16[1,2,64,2048]{3,2,1,0:T(8,128)(2,1)}, bf16[1,2,64,2048]{3,2,1,0:T(8,128)(2,1)S(1)}, u32[]{:S(2)}, u32[]{:S(2)}) %collective-permute-start.1) | collective-permute-done | bytes 524320 | tf_op jit(solution)/shard_map/ppermute | solution.py:13
  74.1 0.1 fusion.26
  74.2 5.7 %convolution_bitcast_fusion = f32[2,1,2,64,2048]{4,3,2,0,1:T(8,128)S(1)} fusion(bf16[2048,2048,1,1]{1,0,3,2:T(8,128)(2,1)} %constant.110, bf16[1,1,2,64,2048]{4,3,2,0,1:T(8,128)(2,1)S(1)} %bitcast.84, bf16[1,1,2,64,2048]{4,3,2,0,1:T(8,128)(2,1)S(1)} %bitcast.76), kind=kOutput, calls=%fused_computation.1 | convolution fusion | flops 2148007936 | bytes 11534336 | tf_op jit(solution)/shard_map/dot_general | solution.py:53
  80.0 8.0 %fusion.18 = (f32[2,1,1,64,2048]{4,3,2,0,1:T(8,128)S(1)}, f32[2,1,1,64,2048]{4,3,2,0,1:T(8,128)S(1)}, f32[2,1,1,64,2048]{4,3,2,0,1:T(8,128)S(1)}, f32[2,1,1,64,2048]{4,3,2,0,1:T(8,128)S(1)}) fusion(f32[2,1,2,64,2048]{4,3,2,0,1:T(8,128)S(1)} %fusion.26, f32[2]{0:T(128)S(1)} %maximum_bitcast_fusion.1, f32[64,2048]{1,0:T(8,128)S(1)} %get-tuple-element.19, ...), kind=kLoop, calls=%fused_computation.33 | loop fusion | flops 3670016 | bytes 9437192 | tf_op jit(solution)/shard_map/sub | solution.py:37
  88.0 0.1 maximum_reduce_fusion.2
  88.1 0.1 maximum_reduce_fusion.3
  88.2 0.1 pad_maximum_fusion.3
  88.3 1.5 %copy.39 = bf16[1,2,64,2048,2]{2,4,3,1,0:T(2,128)(2,1)S(1)} copy(bf16[1,2,64,2048,2]{3,2,1,4,0:T(8,128)(2,1)S(1)} %pad_maximum_fusion.3) | data formatting | bytes 2097152 | tf_op jit(solution)/shard_map/stack | solution.py:48
  89.8 0.8 copy.40
  90.7 0.6 gather_fusion
  91.3 0.1 copy.51
  91.4 30.2 %all_to_all.28 = bf16[4,2,1,2,512,64]{4,5,3,2,1,0:T(8,128)(2,1)S(1)} all-to-all(bf16[4,2,1,2,512,64]{4,5,3,2,1,0:T(8,128)(2,1)S(1)} %bitcast.72), channel_id=1, replica_groups=mesh['swath'=2,'sub'=4,'beam'=2,'half'=2] {'sub'}, dimensions={0} | all-to-all | bytes 2097152 | tf_op jit(solution)/shard_map/all_to_all | solution.py:120
  121.6 0.1 copy.42
  121.7 15.6 %all_to_all.29 = bf16[4,2,1,2,512,64]{4,5,3,2,0,1:T(8,128)(2,1)S(1)} all-to-all(bf16[4,2,1,2,512,64]{4,5,3,2,0,1:T(8,128)(2,1)S(1)} %copy.42), channel_id=1, replica_groups=mesh['swath'=2,'sub'=4,'beam'=2,'half'=2] {'beam'}, dimensions={1} | all-to-all | bytes 2097152 | tf_op jit(solution)/shard_map/all_to_all | solution.py:119
  137.3 0.1 copy.43
  137.4 0.1 copy.44
  137.5 1.3 copy.45
  (5 shorter events, 0.0 us)
Async XLA Ops:
  0.0 7.5 %copy-start = (f32[4]{0:T(128)S(1)}, f32[4]{0:T(128)}, u32[]{:S(2)}) copy-start(f32[4]{0:T(128)} %param.6) | copy-start | bytes 52
  3.3 18.7 %all-to-all-start = ((bf16[1,2,512,512]{3,1,0,2:T(2,128)(2,1)}), bf16[1,2,512,512]{3,1,0,2:T(2,128)(2,1)S(1)}, u32[]{:S(2)}, u32[]{:S(2)}) async-start(bf16[1,2,512,512]{3,1,0,2:T(2,128)(2,1)} %copy.34), calls=%async_computation | async-start | bytes 2097152 | tf_op jit(solution)/shard_map/all_to_all | solution.py:102
  23.0 6.6 %copy-start.1 = (s32[2,4]{1,0:T(2,128)S(1)}, s32[2,4]{1,0:T(2,128)}, u32[]{:S(2)}) copy-start(s32[2,4]{1,0:T(2,128)} %param.7) | copy-start | bytes 100
  23.9 13.2 %collective-permute-start = (bf16[1,2,128,1024]{3,2,1,0:T(8,128)(2,1)S(1)}, bf16[1,2,128,1024]{3,2,1,0:T(8,128)(2,1)S(1)}, u32[]{:S(2)}, u32[]{:S(2)}) collective-permute-start(bf16[1,2,128,1024]{3,2,1,0:T(8,128)(2,1)S(1)} %get-tuple-element.16), channel_id=1, source_target_pairs={{0,4},{4,0},{8,12},{12,8},{1,5},{5,1},{9,13},{13,9},{2,6},{6,2},{1... | collective-permute-start | bytes 1572872 | tf_op jit(solution)/shard_map/ppermute | solution.py:13
  29.6 7.6 %copy-start.2 = (bf16[1024,1024,1,1]{1,0,3,2:T(8,128)(2,1)S(1)}, bf16[1024,1024,1,1]{1,0,3,2:T(8,128)(2,1)}, u32[]{:S(2)}) copy-start(bf16[1024,1024,1,1]{1,0,3,2:T(8,128)(2,1)} %constant.109) | copy-start | bytes 6291460
  49.5 24.6 %collective-permute-start.1 = (bf16[1,2,64,2048]{3,2,1,0:T(8,128)(2,1)}, bf16[1,2,64,2048]{3,2,1,0:T(8,128)(2,1)S(1)}, u32[]{:S(2)}, u32[]{:S(2)}) collective-permute-start(bf16[1,2,64,2048]{3,2,1,0:T(8,128)(2,1)} %copy.48), channel_id=1, source_target_pairs={{0,8},{4,12},{8,0},{12,4},{1,9},{5,13},{9,1},{13,5},{2,10},{6,14},... | collective-permute-start | bytes 1572872 | tf_op jit(solution)/shard_map/ppermute | solution.py:13
where the time goes:
time: 139 us
  blocking collectives  45.8 us (33%)
  waiting for transfers between devices  42.3 us (30%)
  other arithmetic  18.8 us (14%)
  local copies, waits for them, and re-layouts  13.5 us (10%)
  starting transfers between devices  8.68 us (6%)
  matrix products  7.03 us (5%)
  between operations  2.69 us (2%)
    all_to_all x1, blocking collectives, body(): lax.all_to_all(outgoing, 'sub', split_axis=0, concat_axis=0, tiled=True)  30.2 us
    ppermute x2, waiting for transfers between devices, swapped(): lax.ppermute(value, axis, [(i, i ^ 1 << distance) for i in range(lax.axis...  28.6 us
    sub x2, other arithmetic, steer_phase(): real_part * cosine - imag_part * sines  16 us
    all_to_all x1, blocking collectives, body(): lax.all_to_all(lax.all_to_all(outgoing, 'sub', split_axis=0, concat_axis=...  15.6 us
    all_to_all x1, waiting for transfers between devices, body(): lax.all_to_all(images, 'beam', split_axis=2, concat_axis=3, tiled=True)  13.7 us
    dot_general x2, matrix products, odd_local(): jnp.dot(children.reshape(-1, children.shape[-1]), kernel, preferred_eleme...  7.03 us
    ppermute x2, starting transfers between devices, swapped(): lax.ppermute(value, axis, [(i, i ^ 1 << distance) for i in range(lax.axis...  4.45 us
    unnamed x8, local copies, waits for them, and re-layouts  4.43 us
  transfers between devices with their start and end apart: 3, of which 3 were waited for; matrix products, arithmetic and copies ran while one was open for 2% of the time, Pallas kernels for 0%

commit v1 on v0

--- a/solution.py
+++ b/solution.py
@@ -7,6 +7,22 @@
 
 B = 1024
 NR = 1024
+
+
+def swapped_with_each(x, axis, split, join):
+    ways, here = (lax.axis_size(axis), lax.axis_index(axis))
+    width = x.shape[split] // ways
+    lengths = list(x.shape)
+    lengths[split] = width
+    height = lengths[join]
+    lengths[join] = height * ways
+    full = jnp.zeros(lengths, x.dtype)
+    for mask in range(ways):
+        part = lax.dynamic_slice_in_dim(x, (here ^ mask) * width, width, axis=split)
+        if mask:
+            part = lax.ppermute(part, axis, [(d, d ^ mask) for d in range(ways)])
+        full = lax.dynamic_update_slice_in_dim(full, part, (here ^ mask) * height, axis=join)
+    return full
 
 
 def swapped(value, axis, distance):
@@ -117,11 +133,7 @@
     picked = sector_tiles[:, :, :, beam_ids, owners, :]
     outgoing = picked.transpose(4, 3, 0, 1, 5, 2)
     received = lax.all_to_all(
-        lax.all_to_all(outgoing, "sub", split_axis=0, concat_axis=0, tiled=True),
-        "beam",
-        split_axis=1,
-        concat_axis=1,
-        tiled=True,
+        swapped_with_each(outgoing, "sub", 0, 0), "beam", split_axis=1, concat_axis=1, tiled=True
     )
     sector_width = received.shape[4]
     received = received.reshape(

time: 139 us -> 134 us (0.964)
  the two profiles are of different devices: /device:TPU:0 before, /device:TPU:12 now
where the time goes in v1:
time: 134 us; the launch traced here: 133 us
  waiting for transfers between devices  64.5 us (48%)
  other arithmetic  18.7 us (14%)
  blocking collectives  15.7 us (12%)
  local copies, waits for them, and re-layouts  13.8 us (10%)
  starting transfers between devices  10.7 us (8%)
  matrix products  7.03 us (5%)
  between operations  2.95 us (2%)
    ppermute x2, waiting for transfers between devices, swapped(): lax.ppermute(value, axis, [(i, i ^ 1 << distance) for i in range(lax.axis...  28.6 us
    ppermute x3, waiting for transfers between devices, swapped_with_each(): part = lax.ppermute(part, axis, [(d, d ^ mask) for d in range(ways)])  22.8 us
    sub x2, other arithmetic, steer_phase(): real_part * cosine - imag_part * sines  16 us
    all_to_all x1, blocking collectives, body(): lax.all_to_all(swapped_with_each(outgoing, 'sub', 0, 0), 'beam', split_ax...  15.7 us
    all_to_all x1, waiting for transfers between devices, body(): lax.all_to_all(images, 'beam', split_axis=2, concat_axis=3, tiled=True)  13 us
    dot_general x2, matrix products, odd_local(): jnp.dot(children.reshape(-1, children.shape[-1]), kernel, preferred_eleme...  7.03 us
    unnamed x8, local copies, waits for them, and re-layouts  4.43 us
    ppermute x3, starting transfers between devices, swapped_with_each(): part = lax.ppermute(part, axis, [(d, d ^ mask) for d in range(ways)])  3.97 us
  transfers between devices with their start and end apart: 6, of which 6 were waited for; matrix products, arithmetic and copies ran while one was open for 2% of the time, Pallas kernels for 0%

profile of v1, /device:TPU:12, one launch (start us, length us, event | category | flops | bytes accessed | tf_op | source)
XLA Modules:
  0.0 133.2 jit_solution(13610771215091737297)
XLA Ops:
  0.0 0.0 copy-start
  0.0 3.3 %copy.33 = bf16[1,2,512,512]{3,1,0,2:T(2,128)(2,1)} copy(bf16[1,2,512,512]{3,2,1,0:T(8,128)(2,1)} %param.5) | data formatting | bytes 2097152 | tf_op args[0]
  3.3 3.6 %all-to-all-start = ((bf16[1,2,512,512]{3,1,0,2:T(2,128)(2,1)}), bf16[1,2,512,512]{3,1,0,2:T(2,128)(2,1)S(1)}, u32[]{:S(2)}, u32[]{:S(2)}) async-start(bf16[1,2,512,512]{3,1,0,2:T(2,128)(2,1)} %copy.33), calls=%async_computation | async-start | bytes 2097152 | tf_op jit(solution)/shard_map/all_to_all | solution.py:118
  7.0 0.0 copy-done
  7.0 0.7 fusion.34
  7.7 13.0 %all-to-all-done = bf16[1,2,512,512]{3,1,0,2:T(2,128)(2,1)S(1)} async-done(((bf16[1,2,512,512]{3,1,0,2:T(2,128)(2,1)}), bf16[1,2,512,512]{3,1,0,2:T(2,128)(2,1)S(1)}, u32[]{:S(2)}, u32[]{:S(2)}) %all-to-all-start) | async-done | bytes 1048608 | tf_op jit(solution)/shard_map/all_to_all | solution.py:118
  20.7 1.1 copy.51
  21.8 0.0 copy-start.1
  21.8 0.9 all_to_all.19
  22.8 0.1 dynamic-slice_bitcast_fusion
  22.9 0.5 collective-permute-start
  23.4 1.3 maximum_bitcast_fusion
  27.2 0.0 copy-done.1
  27.2 0.0 copy-start.2
  27.3 0.1 broadcast_multiply_fusion.3
  27.4 8.3 %collective-permute-done = bf16[1,2,128,1024]{3,2,1,0:T(8,128)(2,1)S(1)} collective-permute-done((bf16[1,2,128,1024]{3,2,1,0:T(8,128)(2,1)S(1)}, bf16[1,2,128,1024]{3,2,1,0:T(8,128)(2,1)S(1)}, u32[]{:S(2)}, u32[]{:S(2)}) %collective-permute-start) | collective-permute-done | bytes 524320 | tf_op jit(solution)/shard_map/ppermute | solution.py:29
  35.7 0.1 fusion.27
  35.9 0.0 copy-done.2
  35.9 1.3 convolution_bitcast_fusion.1
  37.2 8.0 %fusion.22 = (f32[2,1,1,128,1024]{4,3,2,0,1:T(8,128)S(1)}, f32[2,1,1,128,1024]{4,3,2,0,1:T(8,128)S(1)}, f32[2,1,1,128,1024]{4,3,2,0,1:T(8,128)S(1)}, f32[2,1,1,128,1024]{4,3,2,0,1:T(8,128)S(1)}) fusion(f32[2,1,2,128,1024]{4,3,2,0,1:T(8,128)S(1)} %fusion.27, f32[2]{0:T(128)S(1)} %maximum_bitcast_fusion, f32[128,1024]{1,0:T(8,128)S(1)} %get-tuple-element.32, ...), kind=kLoop, calls=%fused_computation.37 | loop fusion | flops 3670016 | bytes 9437192 | tf_op jit(solution)/shard_map/sub | solution.py:53
  45.2 0.1 maximum_reduce_fusion
  45.3 0.1 maximum_reduce_fusion.1
  45.5 0.1 pad_maximum_fusion.1
  45.6 0.8 copy.35
  46.4 0.6 constant_dynamic-slice_fusion.1
  47.0 1.1 copy.49
  48.2 2.6 %collective-permute-start.1 = (bf16[1,2,64,2048]{3,2,1,0:T(8,128)(2,1)}, bf16[1,2,64,2048]{3,2,1,0:T(8,128)(2,1)S(1)}, u32[]{:S(2)}, u32[]{:S(2)}) collective-permute-start(bf16[1,2,64,2048]{3,2,1,0:T(8,128)(2,1)} %copy.49), channel_id=1, source_target_pairs={{0,8},{4,12},{8,0},{12,4},{1,9},{5,13},{9,1},{13,5},{2,10},{6,14},... | collective-permute-start | bytes 1572872 | tf_op jit(solution)/shard_map/ppermute | solution.py:29
  50.8 0.1 maximum_bitcast_fusion.1
  50.8 0.1 reshape.414
  50.9 0.2 broadcast_multiply_fusion.1
  51.1 0.3 copy.36
  51.4 20.3 %collective-permute-done.1 = bf16[1,2,64,2048]{3,2,1,0:T(8,128)(2,1)S(1)} collective-permute-done((bf16[1,2,64,2048]{3,2,1,0:T(8,128)(2,1)}, bf16[1,2,64,2048]{3,2,1,0:T(8,128)(2,1)S(1)}, u32[]{:S(2)}, u32[]{:S(2)}) %collective-permute-start.1) | collective-permute-done | bytes 524320 | tf_op jit(solution)/shard_map/ppermute | solution.py:29
  71.7 0.1 fusion.26
  71.8 5.7 %convolution_bitcast_fusion = f32[2,1,2,64,2048]{4,3,2,0,1:T(8,128)S(1)} fusion(bf16[2048,2048,1,1]{1,0,3,2:T(8,128)(2,1)} %constant.114, bf16[1,1,2,64,2048]{4,3,2,0,1:T(8,128)(2,1)S(1)} %bitcast.109, bf16[1,1,2,64,2048]{4,3,2,0,1:T(8,128)(2,1)S(1)} %bitcast.101), kind=kOutput, calls=%fused_computation.1 | convolution fusion | flops 2148007936 | bytes 11534336 | tf_op jit(solution)/shard_map/dot_general | solution.py:69
  77.6 8.0 %fusion.18 = (f32[2,1,1,64,2048]{4,3,2,0,1:T(8,128)S(1)}, f32[2,1,1,64,2048]{4,3,2,0,1:T(8,128)S(1)}, f32[2,1,1,64,2048]{4,3,2,0,1:T(8,128)S(1)}, f32[2,1,1,64,2048]{4,3,2,0,1:T(8,128)S(1)}) fusion(f32[2,1,2,64,2048]{4,3,2,0,1:T(8,128)S(1)} %fusion.26, f32[2]{0:T(128)S(1)} %maximum_bitcast_fusion.1, f32[64,2048]{1,0:T(8,128)S(1)} %get-tuple-element.22, ...), kind=kLoop, calls=%fused_computation.33 | loop fusion | flops 3670016 | bytes 9437192 | tf_op jit(solution)/shard_map/sub | solution.py:53
  85.6 0.1 maximum_reduce_fusion.2
  85.7 0.1 maximum_reduce_fusion.3
  85.8 0.1 pad_maximum_fusion.3
  85.9 1.5 %copy.38 = bf16[1,2,64,2048,2]{2,4,3,1,0:T(2,128)(2,1)S(1)} copy(bf16[1,2,64,2048,2]{3,2,1,4,0:T(8,128)(2,1)S(1)} %pad_maximum_fusion.3) | data formatting | bytes 2097152 | tf_op jit(solution)/shard_map/stack | solution.py:64
  87.4 0.8 copy.39
  88.3 0.6 gather_fusion
  88.9 0.1 dynamic-slice_bitcast_fusion.1
  89.0 1.3 collective-permute-start.2
  90.3 2.1 %collective-permute-start.3 = (bf16[1,2,1,2,512,64]{4,5,3,1,0,2:T(8,128)(2,1)S(1)}, bf16[1,2,1,2,512,64]{4,5,3,1,0,2:T(8,128)(2,1)S(1)}, u32[]{:S(2)}, u32[]{:S(2)}) collective-permute-start(bf16[1,2,1,2,512,64]{4,5,3,1,0,2:T(8,128)(2,1)S(1)} %get-tuple-element.14), channel_id=1, source_target_pairs={{0,8},{4,12},{8,0},{12,4},{1,9},{5,13},{9,1},{13,5},{2,10},{6,14},... | collective-permute-start | bytes 786440 | tf_op jit(solution)/shard_map/ppermute | solution.py:23
  92.4 0.1 broadcast_in_dim.6
  92.6 0.6 collective-permute-start.4
  93.1 7.0 %collective-permute-done.2 = bf16[1,2,1,2,512,64]{4,5,3,1,0,2:T(8,128)(2,1)S(1)} collective-permute-done((bf16[1,2,1,2,512,64]{4,5,3,1,0,2:T(8,128)(2,1)S(1)}, bf16[1,2,1,2,512,64]{4,5,3,1,0,2:T(8,128)(2,1)S(1)}, u32[]{:S(2)}, u32[]{:S(2)}) %collective-permute-start.2) | collective-permute-done | bytes 262176 | tf_op jit(solution)/shard_map/ppermute | solution.py:23
  100.2 10.2 %collective-permute-done.3 = bf16[1,2,1,2,512,64]{4,5,3,1,0,2:T(8,128)(2,1)S(1)} collective-permute-done((bf16[1,2,1,2,512,64]{4,5,3,1,0,2:T(8,128)(2,1)S(1)}, bf16[1,2,1,2,512,64]{4,5,3,1,0,2:T(8,128)(2,1)S(1)}, u32[]{:S(2)}, u32[]{:S(2)}) %collective-permute-start.3) | collective-permute-done | bytes 262176 | tf_op jit(solution)/shard_map/ppermute | solution.py:23
  110.4 5.6 %collective-permute-done.4 = bf16[1,2,1,2,512,64]{4,5,3,1,0,2:T(8,128)(2,1)S(1)} collective-permute-done((bf16[1,2,1,2,512,64]{4,5,3,1,0,2:T(8,128)(2,1)S(1)}, bf16[1,2,1,2,512,64]{4,5,3,1,0,2:T(8,128)(2,1)S(1)}, u32[]{:S(2)}, u32[]{:S(2)}) %collective-permute-start.4) | collective-permute-done | bytes 262176 | tf_op jit(solution)/shard_map/ppermute | solution.py:23
  116.0 15.7 %all_to_all.23 = bf16[4,2,1,2,512,64]{4,5,3,2,0,1:T(8,128)(2,1)S(1)} all-to-all(bf16[4,2,1,2,512,64]{4,5,3,2,0,1:T(8,128)(2,1)S(1)} %bitcast_dynamic-update-slice_fusion.1), channel_id=1, replica_groups=mesh['swath'=2,'sub'=4,'beam'=2,'half'=2] {'beam'}, dimensions={1} | all-to-all | bytes 2097152 | tf_op jit(solution)/shard_map/all_to_all | solution.py:135
  131.7 0.1 copy.44
  131.8 0.1 copy.45
  131.9 1.3 copy.46
  (9 shorter events, 0.1 us)
Async XLA Ops:
  0.0 7.0 %copy-start = (f32[4]{0:T(128)S(1)}, f32[4]{0:T(128)}, u32[]{:S(2)}) copy-start(f32[4]{0:T(128)} %param.6) | copy-start | bytes 52
  3.3 17.4 %all-to-all-start = ((bf16[1,2,512,512]{3,1,0,2:T(2,128)(2,1)}), bf16[1,2,512,512]{3,1,0,2:T(2,128)(2,1)S(1)}, u32[]{:S(2)}, u32[]{:S(2)}) async-start(bf16[1,2,512,512]{3,1,0,2:T(2,128)(2,1)} %copy.33), calls=%async_computation | async-start | bytes 2097152 | tf_op jit(solution)/shard_map/all_to_all | solution.py:118
  21.8 5.4 %copy-start.1 = (s32[2,4]{1,0:T(2,128)S(1)}, s32[2,4]{1,0:T(2,128)}, u32[]{:S(2)}) copy-start(s32[2,4]{1,0:T(2,128)} %param.7) | copy-start | bytes 100
  22.9 12.9 %collective-permute-start = (bf16[1,2,128,1024]{3,2,1,0:T(8,128)(2,1)S(1)}, bf16[1,2,128,1024]{3,2,1,0:T(8,128)(2,1)S(1)}, u32[]{:S(2)}, u32[]{:S(2)}) collective-permute-start(bf16[1,2,128,1024]{3,2,1,0:T(8,128)(2,1)S(1)} %get-tuple-element.19), channel_id=1, source_target_pairs={{0,4},{4,0},{8,12},{12,8},{1,5},{5,1},{9,13},{13,9},{2,6},{6,2},{1... | collective-permute-start | bytes 1572872 | tf_op jit(solution)/shard_map/ppermute | solution.py:29
  27.2 8.6 %copy-start.2 = (bf16[1024,1024,1,1]{1,0,3,2:T(8,128)(2,1)S(1)}, bf16[1024,1024,1,1]{1,0,3,2:T(8,128)(2,1)}, u32[]{:S(2)}) copy-start(bf16[1024,1024,1,1]{1,0,3,2:T(8,128)(2,1)} %constant.113) | copy-start | bytes 6291460
  48.2 23.5 %collective-permute-start.1 = (bf16[1,2,64,2048]{3,2,1,0:T(8,128)(2,1)}, bf16[1,2,64,2048]{3,2,1,0:T(8,128)(2,1)S(1)}, u32[]{:S(2)}, u32[]{:S(2)}) collective-permute-start(bf16[1,2,64,2048]{3,2,1,0:T(8,128)(2,1)} %copy.49), channel_id=1, source_target_pairs={{0,8},{4,12},{8,0},{12,4},{1,9},{5,13},{9,1},{13,5},{2,10},{6,14},... | collective-permute-start | bytes 1572872 | tf_op jit(solution)/shard_map/ppermute | solution.py:29
  89.0 11.1 %collective-permute-start.2 = (bf16[1,2,1,2,512,64]{4,5,3,1,0,2:T(8,128)(2,1)S(1)}, bf16[1,2,1,2,512,64]{4,5,3,1,0,2:T(8,128)(2,1)S(1)}, u32[]{:S(2)}, u32[]{:S(2)}) collective-permute-start(bf16[1,2,1,2,512,64]{4,5,3,1,0,2:T(8,128)(2,1)S(1)} %get-tuple-element.15), channel_id=1, source_target_pairs={{0,4},{4,0},{8,12},{12,8},{1,5},{5,1},{9,13},{13,9},{2,6},{6,2},{1... | collective-permute-start | bytes 786440 | tf_op jit(solution)/shard_map/ppermute | solution.py:23
  90.3 20.1 %collective-permute-start.3 = (bf16[1,2,1,2,512,64]{4,5,3,1,0,2:T(8,128)(2,1)S(1)}, bf16[1,2,1,2,512,64]{4,5,3,1,0,2:T(8,128)(2,1)S(1)}, u32[]{:S(2)}, u32[]{:S(2)}) collective-permute-start(bf16[1,2,1,2,512,64]{4,5,3,1,0,2:T(8,128)(2,1)S(1)} %get-tuple-element.14), channel_id=1, source_target_pairs={{0,8},{4,12},{8,0},{12,4},{1,9},{5,13},{9,1},{13,5},{2,10},{6,14},... | collective-permute-start | bytes 786440 | tf_op jit(solution)/shard_map/ppermute | solution.py:23
  92.6 23.5 %collective-permute-start.4 = (bf16[1,2,1,2,512,64]{4,5,3,1,0,2:T(8,128)(2,1)S(1)}, bf16[1,2,1,2,512,64]{4,5,3,1,0,2:T(8,128)(2,1)S(1)}, u32[]{:S(2)}, u32[]{:S(2)}) collective-permute-start(bf16[1,2,1,2,512,64]{4,5,3,1,0,2:T(8,128)(2,1)S(1)} %get-tuple-element.13), channel_id=1, source_target_pairs={{0,12},{4,8},{8,4},{12,0},{1,13},{5,9},{9,5},{13,1},{2,14},{6,10},... | collective-permute-start | bytes 786440 | tf_op jit(solution)/shard_map/ppermute | solution.py:23
